TPU v7x, 256 devices: a whole 4x4x8 slice. The times are simulated.
256 devices in a mesh: rep: 32 (over z, y_hi, core), fsdp: 8 (over x, y_lo).
Axes of the slice: x: 4, y: 4 (y_hi: 2, y_lo: 2; y = y_hi * 2 + y_lo), z: 8, core: 2. Of those that a mesh axis runs over, the one named last changes fastest.
Arguments:
- hidden: bfloat16 [32768, 7168], P(('rep', 'fsdp')), may hold values from -6 to 6
- grad_out: bfloat16 [32768, 4096], P(('rep', 'fsdp')), may hold values from -24 to 24
- down_weight: bfloat16 [7168, 4096], P('fsdp'), may hold values from -0.0625 to 0.0625
- hash_tiles: bfloat16 [3, 32, 7168], P(None, None, 'fsdp'), may hold values from -1 to 1, as said below
- momentum: float32 [8, 3, 32, 4096], P('fsdp', None, None, 'rep'), may hold values from -6 to 6
- error: float32 [8, 3, 32, 4096], P('fsdp', None, None, 'rep'), may hold values from -6 to 6
Outputs:
- grad_hidden: bfloat16 [32768, 7168], P(('rep', 'fsdp'))
- update: float32 [7168, 4096], P('fsdp', 'rep')
- new_momentum: float32 [8, 3, 32, 4096], P('fsdp', None, None, 'rep')
- new_error: float32 [8, 3, 32, 4096], P('fsdp', None, None, 'rep')
Inputs may be any that keep to these rules, and one draw needn't show every extreme that they name: `hash_tiles`: in every sketch row each hidden unit has exactly one nonzero entry, +1 or -1, in one of the 32 buckets; all other entries are 0.
All inputs are finite; a program needn't handle non-finite values.
Results may differ from a plain program's by a relative error of at most 0.0005.
Values may be sent and summed in bfloat16 or wider, within the bound.
No kernel may reach another device: no remote copies, remote signals or barrier semaphores. Data moves between devices by JAX's collectives and lax.ppermute only.
A program may use at most 128 MiB of HBM per device.

v0:
```python
import math
import jax
import jax.numpy as jnp
from jax import lax
from jax.sharding import PartitionSpec as P

momentum_decay = 0.9
step_size = 0.5


def on_device(hidden, grad_out, down_weight, hash_tiles, momentum, error):
    shards = lax.axis_size("fsdp")
    replicas = lax.axis_size("rep")
    tok_rows = grad_out.shape[0]
    model_width = grad_out.shape[1]
    shard_rows = down_weight.shape[0]
    rows_count = hash_tiles.shape[0]
    buckets = hash_tiles.shape[1]
    sketch_rows = rows_count * buckets
    columns = model_width // replicas
    total_tokens = tok_rows * shards * replicas
    table_scale = math.sqrt(buckets / (shard_rows * total_tokens))
    gathered = lax.all_gather(grad_out, "fsdp", axis=0, tiled=True)
    partial_grads = lax.dot_general(
        gathered, down_weight, (((1,), (1,)), ((), ())), preferred_element_type=jnp.float32
    ).astype(jnp.bfloat16)
    grad_hidden = lax.all_to_all(partial_grads, "fsdp", split_axis=0, concat_axis=1, tiled=True)
    all_hash = lax.all_gather(hash_tiles, "fsdp", axis=2, tiled=True)
    projected = jnp.einsum(
        "kfi,tfi->fkt",
        all_hash.reshape(sketch_rows, shards, shard_rows),
        hidden.reshape(tok_rows, shards, shard_rows),
        preferred_element_type=jnp.float32,
    )
    received = lax.all_to_all(projected, "fsdp", split_axis=0, concat_axis=2, tiled=True)[0]
    split_grads = gathered.reshape(tok_rows * shards, replicas, columns)
    grad_block = split_grads.astype(jnp.float32)
    summed = jnp.einsum("kt,trc->rkc", received, grad_block, precision=lax.Precision.HIGHEST)
    sketch_table = lax.psum_scatter(
        (summed * table_scale).reshape(lax.axis_size("rep") * 1, rows_count, buckets, columns),
        "rep",
        scatter_dimension=0,
        tiled=True,
    )
    new_momentum = momentum_decay * momentum + sketch_table
    accumulated = error + step_size * new_momentum
    hash_float = hash_tiles.astype(jnp.float32)
    update = (
        jnp.einsum("jbi,jbc->ic", hash_float, accumulated[0], precision=lax.Precision.HIGHEST)
        / rows_count
    )
    encoded = jnp.einsum("jbi,ic->jbc", hash_float, update, precision=lax.Precision.HIGHEST)
    new_error = accumulated - encoded[None]
    return (grad_hidden, update, new_momentum, new_error)


def solution(mesh):
    return jax.shard_map(
        on_device,
        mesh=mesh,
        in_specs=(
            P(("rep", "fsdp"), None),
            P(("rep", "fsdp"), None),
            P("fsdp", None),
            P(None, None, "fsdp"),
            P("fsdp", None, None, "rep"),
            P("fsdp", None, None, "rep"),
        ),
        out_specs=(
            P(("rep", "fsdp"), None),
            P("fsdp", "rep"),
            P("fsdp", None, None, "rep"),
            P("fsdp", None, None, "rep"),
        ),
        check_vma=False,
    )
```

profile of v0, /device:TPU:2, one launch (start us, length us, event | category | flops | bytes accessed | tf_op | source)
XLA Modules:
  0.0 371.5 jit_solution(13918211053489265926)
XLA Ops:
  7.2 0.0 all-gather.5.cloned.1.call-start
  7.2 0.7 all-gather.5.cloned.1.call-update
  7.9 0.0 all-gather.3.cloned.1.call-start
  7.9 2.3 copy.13
  10.2 0.0 copy-start.4
  10.2 0.0 all-gather.3.cloned.1.call-update
  10.2 0.0 reduce-scatter.2.cloned.1.call-start
  10.3 46.5 %all-gather.5.cloned.1.call-done = bf16[3,32,7168]{2,1,0:T(8,128)(2,1)} async-done(((bf16[3,32,896]{2,1,0:T(8,128)(2,1)}), bf16[3,32,7168]{2,1,0:T(8,128)(2,1)}) %all-gather.5.cloned.1.call-update) | async-done | bytes 1376272 | tf_op jit(solution)/shard_map/all_gather | solution.py:28
  56.8 1.6 copy.23
  58.4 0.0 copy-done.4
  58.4 0.8 fusion
  59.1 10.5 %all_to_all.34 = f32[8,96,128]{2,1,0:T(8,128)S(1)} all-to-all(f32[8,96,128]{2,1,0:T(8,128)S(1)} %fusion), channel_id=1, replica_groups=mesh['rep'=32,'fsdp'=8] {'fsdp'}, dimensions={0} | all-to-all | bytes 786432 | tf_op jit(solution)/shard_map/all_to_all | solution.py:35
  69.6 0.2 copy.17
  69.9 0.1 reshape.28
  69.9 161.1 %all-gather.3.cloned.1.call-done = bf16[1024,4096]{0,1:T(8,128)(2,1)} async-done(((bf16[128,4096]{0,1:T(8,128)(2,1)}), bf16[1024,4096]{0,1:T(8,128)(2,1)}) %all-gather.3.cloned.1.call-update) | async-done | bytes 8388624 | tf_op jit(solution)/shard_map/all_gather | solution.py:23
  231.1 11.0 %convolution_multiply_fusion = f32[96,32,128]{2,0,1:T(8,128)} fusion(f32[96,1024,1]{1,0,2:T(8,128)S(1)} %reshape.28, bf16[1024,32,128]{0,2,1:T(8,128)(2,1)} %bitcast.43), kind=kOutput, calls=%fused_computation.4 | convolution fusion | flops 4832231424 | bytes 10354688 | tf_op jit(solution)/shard_map/kt,trc->rkc/dot_general | solution.py:38
  242.0 0.0 reduce-scatter.2.cloned.1.call-update
  242.1 13.5 %convolution_convert_fusion = bf16[1024,896]{1,0:T(8,128)(2,1)S(1)} fusion(bf16[1024,4096]{0,1:T(8,128)(2,1)} %all-gather.3.cloned.1.call-done, bf16[896,4096]{1,0:T(8,128)(2,1)} %param.8), kind=kOutput, calls=%fused_computation.3 | convolution fusion | flops 7517110272 | bytes 17563648 | tf_op jit(solution)/shard_map/dot_general | solution.py:24
  255.6 27.9 %all_to_all.35 = bf16[8,128,896]{2,1,0:T(8,128)(2,1)S(1)} all-to-all(bf16[8,128,896]{2,1,0:T(8,128)(2,1)S(1)} %bitcast.48), channel_id=1, replica_groups=mesh['rep'=32,'fsdp'=8] {'fsdp'}, dimensions={0} | all-to-all | bytes 3670016 | tf_op jit(solution)/shard_map/all_to_all | solution.py:27
  283.5 0.0 copy-start.3
  283.5 0.0 copy-start
  283.5 0.0 copy-start.2
  283.5 1.5 copy.22
  285.0 76.7 %reduce-scatter.2.cloned.1.call-done = f32[1,3,32,128]{3,2,1,0:T(8,128)} async-done(((f32[32,3,32,128]{3,2,1,0:T(8,128)}), f32[1,3,32,128]{3,2,1,0:T(8,128)}) %reduce-scatter.2.cloned.1.call-update) | async-done | bytes 49168 | tf_op jit(solution)/shard_map/reduce_scatter | solution.py:39
  361.7 0.0 copy-done.3
  361.7 0.8 multiply_add_fusion.1
  362.6 0.0 copy-done
  362.6 0.0 copy-done.2
  362.6 0.0 copy-start.1
  362.6 0.4 fusion.4
  363.0 1.0 fusion.5
  364.0 1.0 copy.19
  365.0 0.0 copy-done.1
Async XLA Ops:
  7.2 49.6 %all-gather.5.cloned.1.call-start = ((), (), s32[]{:S(2)}) async-start(), calls=%async_computation.4 | async-start | bytes 1548288 | tf_op jit(solution)/shard_map/all_gather | solution.py:28
  7.9 223.2 %all-gather.3.cloned.1.call-start = ((), (), s32[]{:S(2)}) async-start(), calls=%async_computation.3 | async-start | bytes 9437184 | tf_op jit(solution)/shard_map/all_gather | solution.py:23
  10.2 48.1 %copy-start.4 = (bf16[128,7168]{1,0:T(8,128)(2,1)S(1)}, bf16[128,7168]{1,0:T(8,128)(2,1)}, u32[]{:S(2)}) copy-start(bf16[128,7168]{1,0:T(8,128)(2,1)} %param.6) | copy-start | bytes 5505028
  10.2 351.5 %reduce-scatter.2.cloned.1.call-start = ((), (), s32[]{:S(2)}) async-start(), calls=%async_computation.5 | async-start | bytes 1622016 | tf_op jit(solution)/shard_map/reduce_scatter | solution.py:39
  283.5 78.3 %copy-start.3 = (f32[1,3,32,128]{3,2,1,0:T(8,128)S(1)}, f32[1,3,32,128]{3,2,1,0:T(8,128)}, u32[]{:S(2)}) copy-start(f32[1,3,32,128]{3,2,1,0:T(8,128)} %param.10) | copy-start | bytes 147460
  283.5 79.1 %copy-start = (bf16[3,32,896]{2,1,0:T(8,128)(2,1)S(1)}, bf16[3,32,896]{2,1,0:T(8,128)(2,1)}, u32[]{:S(2)}) copy-start(bf16[3,32,896]{2,1,0:T(8,128)(2,1)} %param.9) | copy-start | bytes 516100
  283.5 79.1 %copy-start.2 = (f32[1,3,32,128]{3,2,1,0:T(8,128)S(1)}, f32[1,3,32,128]{3,2,1,0:T(8,128)}, u32[]{:S(2)}) copy-start(f32[1,3,32,128]{3,2,1,0:T(8,128)} %param.11) | copy-start | bytes 147460
  362.6 2.4 copy-start.1
Sparse Core Ops, SparseCore 0:
  9.8 46.9 all-gather.4
  59.1 171.9 all-gather.2
  242.2 119.5 reduce-scatter.1
where the time goes:
time: 372 us
  waiting for transfers between devices  285 us (77%)
  blocking collectives  38.4 us (10%)
  matrix products  26.7 us (7%)
  between operations  13.8 us (4%)
  local copies, waits for them, and re-layouts  6.63 us (2%)
    all_gather x1, waiting for transfers between devices, on_device(): gathered = lax.all_gather(grad_out, 'fsdp', axis=0, tiled=True)  161 us
    reduce_scatter x1, waiting for transfers between devices, on_device(): lax.psum_scatter((summed * table_scale).reshape(lax.axis_size('rep') * 1,...  76.7 us
    all_gather x1, waiting for transfers between devices, on_device(): all_hash = lax.all_gather(hash_tiles, 'fsdp', axis=2, tiled=True)  46.5 us
    all_to_all x1, blocking collectives, on_device(): lax.all_to_all(partial_grads, 'fsdp', split_axis=0, concat_axis=1, tiled=...  27.9 us
    dot_general x1, matrix products, on_device(): lax.dot_general(gathered, down_weight, (((1,), (1,)), ((), ())), preferre...  13.5 us
    dot_general x1, matrix products, on_device(): jnp.einsum('kt,trc->rkc', received, grad_block, precision=lax.Precision.H...  11 us
    all_to_all x1, blocking collectives, on_device(): lax.all_to_all(projected, 'fsdp', split_axis=0, concat_axis=2, tiled=True)  10.5 us
  transfers between devices with their start and end apart: 3, of which 3 were waited for; matrix products, arithmetic and copies ran while one was open for 5% of the time, Pallas kernels for 0%

commit v1 on v0

--- a/solution.py
+++ b/solution.py
@@ -25,7 +25,9 @@
         gathered, down_weight, (((1,), (1,)), ((), ())), preferred_element_type=jnp.float32
     ).astype(jnp.bfloat16)
     grad_hidden = lax.all_to_all(partial_grads, "fsdp", split_axis=0, concat_axis=1, tiled=True)
-    all_hash = lax.all_gather(hash_tiles, "fsdp", axis=2, tiled=True)
+    all_hash = jnp.concatenate(
+        lax.all_to_all(jnp.stack([hash_tiles] * lax.axis_size("fsdp")), "fsdp", 0, 0), axis=2
+    )
     projected = jnp.einsum(
         "kfi,tfi->fkt",
         all_hash.reshape(sketch_rows, shards, shard_rows),

time: 372 us -> 337 us (0.906)
  waiting for transfers between devices: 285 us -> 216 us
  blocking collectives: 38.4 us -> 73.9 us
    all_gather x1 -> x0, waiting for transfers between devices: 46.5 us -> none  [on_device(): all_hash = lax.all_gather(hash_tiles, 'fsdp', axis=2, tiled=True)]
    all_to_all x0 -> x1, blocking collectives: none -> 34.7 us  [on_device(): lax.all_to_all(jnp.stack([hash_tiles] * lax.axis_size('fsdp')), 'fsdp', 0...]
    all_gather x1, waiting for transfers between devices: 161 us -> 138 us  [on_device(): gathered = lax.all_gather(grad_out, 'fsdp', axis=0, tiled=True)]
  transfers between devices with their start and end apart: 3 -> 2, of which waited for: 3 -> 2; matrix products, arithmetic and copies ran while one was open for 5% -> 5% of each run, Pallas kernels for 0% -> 0%
where the time goes in v1:
time: 337 us
  waiting for transfers between devices  216 us (64%)
  blocking collectives  73.9 us (22%)
  matrix products  26.7 us (8%)
  between operations  14.1 us (4%)
  local copies, waits for them, and re-layouts  5.2 us (2%)
    all_gather x1, waiting for transfers between devices, on_device(): gathered = lax.all_gather(grad_out, 'fsdp', axis=0, tiled=True)  138 us
    reduce_scatter x1, waiting for transfers between devices, on_device(): lax.psum_scatter((summed * table_scale).reshape(lax.axis_size('rep') * 1,...  78.1 us
    all_to_all x1, blocking collectives, on_device(): lax.all_to_all(jnp.stack([hash_tiles] * lax.axis_size('fsdp')), 'fsdp', 0...  34.7 us
    all_to_all x1, blocking collectives, on_device(): lax.all_to_all(partial_grads, 'fsdp', split_axis=0, concat_axis=1, tiled=...  27.1 us
    dot_general x1, matrix products, on_device(): lax.dot_general(gathered, down_weight, (((1,), (1,)), ((), ())), preferre...  13.5 us
    all_to_all x1, blocking collectives, on_device(): lax.all_to_all(projected, 'fsdp', split_axis=0, concat_axis=2, tiled=True)  12.1 us
    dot_general x1, matrix products, on_device(): jnp.einsum('kt,trc->rkc', received, grad_block, precision=lax.Precision.H...  11 us
  transfers between devices with their start and end apart: 2, of which 2 were waited for; matrix products, arithmetic and copies ran while one was open for 5% of the time, Pallas kernels for 0%

profile of v1, /device:TPU:2, one launch (start us, length us, event | category | flops | bytes accessed | tf_op | source)
XLA Modules:
  0.0 336.7 jit_solution(13446011573906868605)
XLA Ops:
  7.2 0.0 copy-start
  7.2 0.0 all-gather.2.cloned.1.call-start
  7.2 2.3 copy.13
  9.5 0.0 all-gather.2.cloned.1.call-update
  9.5 0.0 copy-start.4
  9.6 0.0 reduce-scatter.2.cloned.1.call-start
  9.6 0.0 copy-done
  9.6 0.1 stack.2
  9.7 34.7 %all_to_all.39 = bf16[8,3,32,896]{3,2,1,0:T(8,128)(2,1)S(1)} all-to-all(bf16[8,3,32,896]{3,2,1,0:T(8,128)(2,1)S(1)} %stack.2), channel_id=1, replica_groups=mesh['rep'=32,'fsdp'=8] {'fsdp'}, dimensions={0} | all-to-all | bytes 2752512 | tf_op jit(solution)/shard_map/all_to_all | solution.py:29
  44.4 0.0 copy-done.4
  44.4 0.8 fusion
  45.2 12.1 %all_to_all.40 = f32[8,96,128]{2,1,0:T(8,128)S(1)} all-to-all(f32[8,96,128]{2,1,0:T(8,128)S(1)} %fusion), channel_id=1, replica_groups=mesh['rep'=32,'fsdp'=8] {'fsdp'}, dimensions={0} | all-to-all | bytes 786432 | tf_op jit(solution)/shard_map/all_to_all | solution.py:37
  57.3 0.2 copy.16
  57.5 0.1 reshape.30
  57.6 137.9 %all-gather.2.cloned.1.call-done = bf16[1024,4096]{0,1:T(8,128)(2,1)} async-done(((bf16[128,4096]{0,1:T(8,128)(2,1)}), bf16[1024,4096]{0,1:T(8,128)(2,1)}) %all-gather.2.cloned.1.call-update) | async-done | bytes 8388624 | tf_op jit(solution)/shard_map/all_gather | solution.py:23
  195.5 11.0 %convolution_multiply_fusion = f32[96,32,128]{2,0,1:T(8,128)} fusion(f32[96,1024,1]{1,0,2:T(8,128)S(1)} %reshape.30, bf16[1024,32,128]{0,2,1:T(8,128)(2,1)} %bitcast.44), kind=kOutput, calls=%fused_computation.4 | convolution fusion | flops 4832231424 | bytes 10354688 | tf_op jit(solution)/shard_map/kt,trc->rkc/dot_general | solution.py:40
  206.4 0.0 reduce-scatter.2.cloned.1.call-update
  206.5 13.5 %convolution_convert_fusion = bf16[1024,896]{1,0:T(8,128)(2,1)S(1)} fusion(bf16[1024,4096]{0,1:T(8,128)(2,1)} %all-gather.2.cloned.1.call-done, bf16[896,4096]{1,0:T(8,128)(2,1)} %param.8), kind=kOutput, calls=%fused_computation.3 | convolution fusion | flops 7517110272 | bytes 17563648 | tf_op jit(solution)/shard_map/dot_general | solution.py:24
  220.0 27.1 %all_to_all.41 = bf16[8,128,896]{2,1,0:T(8,128)(2,1)S(1)} all-to-all(bf16[8,128,896]{2,1,0:T(8,128)(2,1)S(1)} %bitcast.49), channel_id=1, replica_groups=mesh['rep'=32,'fsdp'=8] {'fsdp'}, dimensions={0} | all-to-all | bytes 3670016 | tf_op jit(solution)/shard_map/all_to_all | solution.py:27
  247.1 0.0 copy-start.3
  247.1 0.0 copy-start.2
  247.1 1.5 copy.21
  248.6 78.1 %reduce-scatter.2.cloned.1.call-done = f32[1,3,32,128]{3,2,1,0:T(8,128)} async-done(((f32[32,3,32,128]{3,2,1,0:T(8,128)}), f32[1,3,32,128]{3,2,1,0:T(8,128)}) %reduce-scatter.2.cloned.1.call-update) | async-done | bytes 49168 | tf_op jit(solution)/shard_map/reduce_scatter | solution.py:41
  326.7 0.0 copy-done.3
  326.7 0.8 multiply_add_fusion.1
  327.5 0.0 copy-done.2
  327.5 0.0 copy-start.1
  327.5 0.4 fusion.3
  327.9 1.0 fusion.4
  328.9 1.0 copy.18
  329.9 0.0 copy-done.1
Async XLA Ops:
  7.2 2.4 copy-start
  7.2 188.3 %all-gather.2.cloned.1.call-start = ((), (), s32[]{:S(2)}) async-start(), calls=%async_computation.4 | async-start | bytes 9437184 | tf_op jit(solution)/shard_map/all_gather | solution.py:23
  9.5 34.9 %copy-start.4 = (bf16[128,7168]{1,0:T(8,128)(2,1)S(1)}, bf16[128,7168]{1,0:T(8,128)(2,1)}, u32[]{:S(2)}) copy-start(bf16[128,7168]{1,0:T(8,128)(2,1)} %param.6) | copy-start | bytes 5505028
  9.6 317.1 %reduce-scatter.2.cloned.1.call-start = ((), (), s32[]{:S(2)}) async-start(), calls=%async_computation.5 | async-start | bytes 1622016 | tf_op jit(solution)/shard_map/reduce_scatter | solution.py:41
  247.1 79.6 %copy-start.3 = (f32[1,3,32,128]{3,2,1,0:T(8,128)S(1)}, f32[1,3,32,128]{3,2,1,0:T(8,128)}, u32[]{:S(2)}) copy-start(f32[1,3,32,128]{3,2,1,0:T(8,128)} %param.10) | copy-start | bytes 147460
  247.1 80.4 %copy-start.2 = (f32[1,3,32,128]{3,2,1,0:T(8,128)S(1)}, f32[1,3,32,128]{3,2,1,0:T(8,128)}, u32[]{:S(2)}) copy-start(f32[1,3,32,128]{3,2,1,0:T(8,128)} %param.11) | copy-start | bytes 147460
  327.5 2.4 copy-start.1
Sparse Core Ops, SparseCore 0:
  10.3 185.1 all-gather.1
  206.6 120.0 reduce-scatter.1
